TPU v7x, 512 devices: a whole 4x8x8 slice. The times are simulated.
512 devices in a mesh: seq: 128 (over y, z, core), tp: 4 (over x).
Axes of the slice: x: 4, y: 8, z: 8, core: 2. Of those that a mesh axis runs over, the one named last changes fastest.
Arguments:
- tokens: bfloat16 [32768, 1280], P('seq', 'tp'), may hold values from -6 to 6
- first_gain: float32 [1280], replicated, may hold values from 0.1 to 1.9
- w_query: bfloat16 [1280, 1280], P(None, 'tp')
- w_key: bfloat16 [1280, 1280], P(None, 'tp')
- w_value: bfloat16 [1280, 1280], P(None, 'tp'), may hold values from -0.15625 to 0.15625
- w_out: bfloat16 [1280, 1280], P('tp'), may hold values from -0.625 to 0.625
- segment_ids: int32 [32768], P('seq'), may hold values from 0 to 191, never falling along the last dimension, each value on 1 to 512 neighbouring positions
- keep_mask: int32 [32768], P('seq'), may hold values 0 or 1
- merge_gain: float32 [1280], replicated, may hold values from 0.1 to 1.9
- w_merge: bfloat16 [5120, 640], P('tp'), may hold values from -0.078125 to 0.078125
- merge_index: int32 [8192, 4], P('seq'), may hold values from 0 to 32767, as said below
- destination: int32 [8192], P('seq'), may hold values from 0 to 8191, as said below
Outputs:
- delivered: bfloat16 [8192, 640], P('seq', 'tp')
Inputs may be any that keep to these rules, and one draw needn't show every extreme that they name: `segment_ids`: segment numbers never fall along the tokens; each picture or clip holds 1 to 512 tokens and one holds exactly 512. `merge_index`: the four entries of merged row m are different tokens of the device that holds row m, that is of rows (m // 64) * 256 to that plus 256 - 1; every token lies in exactly one group. `destination`: a permutation of the merged rows. The owner of row m is destination[m] // 64; the 64 rows of each device go to exactly 32 owners, exactly 2 rows to each.
All inputs are finite; a program needn't handle non-finite values. No bound on the sum of `keep_mask` on one device may be relied on, other than what follows from the above.
Results may differ from a plain program's by a relative error of at most 0.022.
Values may be sent and summed in bfloat16 or wider, within the bound.
No kernel may reach another device: no remote copies, remote signals or barrier semaphores. Data moves between devices by JAX's collectives and lax.ppermute only.
A program may use at most 64 MiB of HBM per device.

v0:
```python
import jax
import jax.numpy as jnp
from jax import lax
from jax.sharding import PartitionSpec as P

HD = 80
CAP = 2
EPS = 1e-06


def from_behind(shard, axis, by):
    length = lax.axis_size(axis)
    pairs = [(i, i + by) for i in range(length) if 0 <= i + by < length]
    return lax.ppermute(shard, axis, pairs)


def layer_norm(activations, norm_gain):
    activations = activations.astype(jnp.float32)
    row_mean = jnp.mean(activations, axis=-1, keepdims=True)
    centered = activations - row_mean
    variance = jnp.mean(centered * centered, axis=-1, keepdims=True)
    return centered * lax.rsqrt(variance + EPS) * norm_gain


def body(
    tokens,
    first_gain,
    w_query,
    w_key,
    w_value,
    w_out,
    segment_ids,
    keep_mask,
    merge_gain,
    w_merge,
    merge_index,
    destination,
):
    row_count = tokens.shape[0]
    local_width = w_query.shape[1]
    heads_here = local_width // HD
    tp_size = lax.axis_size("tp")
    seq_size = lax.axis_size("seq")
    gathered = lax.all_gather(tokens, "tp", axis=1, tiled=True)
    normed = layer_norm(gathered, first_gain).astype(jnp.bfloat16)
    queries = jnp.dot(normed, w_query, preferred_element_type=jnp.float32).astype(jnp.bfloat16)
    key_rows = jnp.dot(normed, w_key, preferred_element_type=jnp.float32).astype(jnp.bfloat16)
    value_rows = jnp.dot(normed, w_value, preferred_element_type=jnp.float32).astype(jnp.bfloat16)
    paired = jnp.concatenate([key_rows, value_rows], axis=1)
    code_query = segment_ids + 1
    code_key = jnp.where(keep_mask > 0, code_query, 0)
    pair_list = [paired]
    code_list = [code_key]
    for offset in (1, 2, -1, -2):
        moved_pair, moved_code = from_behind((paired, code_key), "seq", offset)
        pair_list.append(moved_pair)
        code_list.append(moved_code)
    all_pairs = jnp.concatenate(pair_list, axis=0)
    all_codes = jnp.concatenate(code_list, axis=0)
    window = all_pairs.shape[0]
    key_heads = all_pairs[:, :local_width].reshape(window, heads_here, HD)
    value_heads = all_pairs[:, local_width:].reshape(window, heads_here, HD)
    query_heads = queries.reshape(row_count, heads_here, HD)
    score_scale = HD ** (-0.5)
    scores = (
        jnp.einsum("qhd,khd->hqk", query_heads, key_heads, preferred_element_type=jnp.float32)
        * score_scale
    )
    query_pos = jnp.arange(row_count)[:, None]
    key_pos = jnp.arange(window)[None, :]
    allowed = (code_query[:, None] == all_codes[None, :]) | (key_pos == query_pos)
    scores = jnp.where(allowed[None], scores, -1e30)
    row_max = jnp.max(scores, axis=-1, keepdims=True)
    exponent = jnp.exp(scores - row_max)
    row_total = jnp.sum(exponent, axis=-1, keepdims=True)
    weights = (exponent / row_total).astype(jnp.bfloat16)
    attended = jnp.einsum("hqk,khd->qhd", weights, value_heads, preferred_element_type=jnp.float32)
    attended = attended.reshape(row_count, local_width).astype(jnp.bfloat16)
    position = lax.axis_index("tp")
    seq_index = lax.axis_index("seq")
    local_index = merge_index - seq_index * row_count
    order = local_index.T.reshape(row_count)
    attended_sorted = jnp.take(attended, order, axis=0)
    partial_sum = jnp.dot(attended_sorted, w_out, preferred_element_type=jnp.float32)
    mixed_sum = lax.psum_scatter(
        partial_sum.astype(jnp.bfloat16), "tp", scatter_dimension=0, tiled=True
    ).astype(jnp.float32)
    column = lax.dynamic_slice_in_dim(local_index, position, 1, 1)[:, 0]
    residual = jnp.take(gathered, column, axis=0)
    updated = residual.astype(jnp.float32) + mixed_sum
    picked = layer_norm(updated, merge_gain).astype(jnp.bfloat16)
    partial_proj = jnp.dot(picked, w_merge, preferred_element_type=jnp.float32)
    projected = lax.psum_scatter(
        partial_proj.astype(jnp.bfloat16), "tp", scatter_dimension=1, tiled=True
    )
    slot_count = projected.shape[0]
    width = projected.shape[1]
    owner = destination // slot_count
    slot = destination - owner * slot_count
    lane = jnp.arange(slot_count)
    same_owner = owner[:, None] == owner[None, :]
    earlier = lane[None, :] < lane[:, None]
    rank = jnp.sum(jnp.where(same_owner & earlier, 1, 0), axis=1)
    send_pos = owner * CAP + rank
    target = jnp.arange(seq_size * CAP)
    send_hot = (send_pos[None, :] == target[:, None]).astype(jnp.bfloat16)
    send_rows = jnp.dot(send_hot, projected, preferred_element_type=jnp.float32)
    send_rows = send_rows.astype(jnp.bfloat16).reshape(seq_size, CAP, width)
    slot_code = (slot + 1).astype(jnp.float32)
    send_slot = jnp.dot(send_hot.astype(jnp.float32), slot_code, precision=lax.Precision.HIGHEST)
    slot_row = jnp.zeros((seq_size, 1, width), jnp.bfloat16)
    slot_row = slot_row.at[:, 0, :CAP].set(send_slot.reshape(seq_size, CAP).astype(jnp.bfloat16))
    send_buf = jnp.concatenate([send_rows, slot_row], axis=1).reshape(seq_size * (CAP + 1), width)
    recv = lax.all_to_all(send_buf, "seq", 0, 0, tiled=True).reshape(seq_size, CAP + 1, width)
    recv_rows = recv[:, :CAP, :].reshape(seq_size * CAP, width)
    recv_slot = recv[:, CAP, :CAP].reshape(seq_size * CAP).astype(jnp.int32) - 1
    recv_hot = (recv_slot[None, :] == lane[:, None]).astype(jnp.bfloat16)
    delivered = jnp.dot(recv_hot, recv_rows, preferred_element_type=jnp.float32)
    return delivered.astype(jnp.bfloat16)


def solution(mesh):
    return jax.shard_map(
        body,
        mesh=mesh,
        in_specs=(
            P("seq", "tp"),
            P(),
            P(None, "tp"),
            P(None, "tp"),
            P(None, "tp"),
            P("tp", None),
            P("seq"),
            P("seq"),
            P(),
            P("tp", None),
            P("seq", None),
            P("seq"),
        ),
        out_specs=P("seq", "tp"),
        check_vma=False,
    )
```

profile of v0, /device:TPU:1, one launch (start us, length us, event | category | flops | bytes accessed | tf_op | source)
XLA Modules:
  0.0 177.3 jit_solution(7128493967322918882)
XLA Ops:
  6.5 11.7 %all_gather.3 = bf16[256,1280]{0,1:T(8,128)(2,1)S(1)} all-gather(bf16[256,320]{0,1:T(8,128)(2,1)} %param.14), channel_id=1, replica_groups=mesh['seq'=128,'tp'=4] {'tp'}, dimensions={1}, use_global_device_ids=true | all-gather | bytes 819200 | tf_op jit(solution)/shard_map/all_gather | solution.py:44
  18.2 0.2 convert_reduce_fusion
  18.4 0.2 fusion.9
  18.7 0.5 convolution_convert_fusion.3
  19.2 0.4 copy-done.9
  19.6 0.5 convolution_convert_fusion.2
  20.1 0.9 pad_maximum_fusion
  20.9 7.4 %collective-permute-start = (bf16[256,640]{0,1:T(8,128)(2,1)}, bf16[256,640]{0,1:T(8,128)(2,1)}, u32[]{:S(2)}, u32[]{:S(2)}) collective-permute-start(bf16[256,640]{0,1:T(8,128)(2,1)} %get-tuple-element.23), channel_id=1, source_target_pairs={{0,4},{4,8},{8,12},{12,16},{16,20},{20,24},{24,28},{28,32},{32,36}... | collective-permute-start | bytes 983048 | tf_op jit(solution)/shard_map/ppermute | solution.py:14
  28.4 4.0 %collective-permute-start.1 = (bf16[256,640]{0,1:T(8,128)(2,1)}, bf16[256,640]{0,1:T(8,128)(2,1)S(1)}, u32[]{:S(2)}, u32[]{:S(2)}) collective-permute-start(bf16[256,640]{0,1:T(8,128)(2,1)} %get-tuple-element.23), channel_id=1, source_target_pairs={{0,8},{4,12},{8,16},{12,20},{16,24},{20,28},{24,32},{28,36},{32,40... | collective-permute-start | bytes 983048 | tf_op jit(solution)/shard_map/ppermute | solution.py:14
  32.4 2.3 %collective-permute-start.2 = (bf16[256,640]{0,1:T(8,128)(2,1)}, bf16[256,640]{0,1:T(8,128)(2,1)S(1)}, u32[]{:S(2)}, u32[]{:S(2)}) collective-permute-start(bf16[256,640]{0,1:T(8,128)(2,1)} %get-tuple-element.23), channel_id=1, source_target_pairs={{4,0},{8,4},{12,8},{16,12},{20,16},{24,20},{28,24},{32,28},{36,32}... | collective-permute-start | bytes 983048 | tf_op jit(solution)/shard_map/ppermute | solution.py:14
  34.7 1.3 collective-permute-start.3
  36.1 3.9 %collective-permute-start.4 = (s32[256]{0:T(256)S(1)}, s32[256]{0:T(256)S(1)}, u32[]{:S(2)}, u32[]{:S(2)}) collective-permute-start(s32[256]{0:T(256)S(1)} %get-tuple-element.20), channel_id=1, source_target_pairs={{0,4},{4,8},{8,12},{12,16},{16,20},{20,24},{24,28},{28,32},{32,36}... | collective-permute-start | bytes 3080 | tf_op jit(solution)/shard_map/ppermute | solution.py:14
  40.2 2.4 %convolution_convert_fusion.1 = bf16[256,320]{0,1:T(8,128)(2,1)} fusion(bf16[1280,320]{0,1:T(8,128)(2,1)} %param.16, bf16[256,1280]{0,1:T(8,128)(2,1)S(1)} %all_gather.3, f32[1280]{0:T(1024)S(1)} %copy-done.10, f32[256]{0:T(256)S(1)} %add_rsqrt_fusion, f32[256]{0:T(256)S(1)} %broadcast_multiply_fusion), kind=kOutput, calls=%fused_computation.23 | convolution fusion | flops 211435520 | bytes 1645568 | tf_op jit(solution)/shard_map/dot_general | solution.py:46
  42.6 4.0 %collective-permute-start.5 = (s32[256]{0:T(256)S(1)}, s32[256]{0:T(256)S(1)}, u32[]{:S(2)}, u32[]{:S(2)}) collective-permute-start(s32[256]{0:T(256)S(1)} %get-tuple-element.20), channel_id=1, source_target_pairs={{0,8},{4,12},{8,16},{12,20},{16,24},{20,28},{24,32},{28,36},{32,40... | collective-permute-start | bytes 3080 | tf_op jit(solution)/shard_map/ppermute | solution.py:14
  46.6 0.7 collective-permute-done.5
  47.3 1.9 %collective-permute-start.6 = (s32[256]{0:T(256)S(1)}, s32[256]{0:T(256)S(1)}, u32[]{:S(2)}, u32[]{:S(2)}) collective-permute-start(s32[256]{0:T(256)S(1)} %get-tuple-element.20), channel_id=1, source_target_pairs={{4,0},{8,4},{12,8},{16,12},{20,16},{24,20},{28,24},{32,28},{36,32}... | collective-permute-start | bytes 3080 | tf_op jit(solution)/shard_map/ppermute | solution.py:14
  49.2 4.0 %collective-permute-done.6 = s32[256]{0:T(256)S(1)} collective-permute-done((s32[256]{0:T(256)S(1)}, s32[256]{0:T(256)S(1)}, u32[]{:S(2)}, u32[]{:S(2)}) %collective-permute-start.6) | collective-permute-done | bytes 1056 | tf_op jit(solution)/shard_map/ppermute | solution.py:14
  53.3 1.3 collective-permute-start.7
  54.6 3.8 %collective-permute-done.7 = s32[256]{0:T(256)S(1)} collective-permute-done((s32[256]{0:T(256)S(1)}, s32[256]{0:T(256)S(1)}, u32[]{:S(2)}, u32[]{:S(2)}) %collective-permute-start.7) | collective-permute-done | bytes 1056 | tf_op jit(solution)/shard_map/ppermute | solution.py:14
  58.3 1.0 fusion.12
  59.3 1.0 constant_dynamic-update-slice_fusion.3
  60.5 1.0 fusion.54
  61.5 2.9 %exponential_reduce_fusion = f32[4,256]{1,0:T(4,128)S(1)} fusion(pred[256,1280]{1,0:T(8,128)(4,1)S(1)} %copy-done.3, bf16[256,4,80]{0,2,1:T(8,128)(2,1)} %bitcast.38, bf16[1280,4,80]{0,2,1:T(8,128)(2,1)S(1)} %bitcast.31), kind=kOutput, calls=%fused_computation.6 | convolution fusion | flops 214959360 | bytes 1314816 | tf_op jit(solution)/shard_map/sub | solution.py:74
  64.4 4.1 %fusion.13 = bf16[4,80,256]{2,1,0:T(8,128)(2,1)} fusion(bf16[1280,4,80]{0,2,1:T(8,128)(2,1)} %bitcast.33, f32[4,256]{1,0:T(4,128)S(1)} %exponential_reduce_fusion, pred[256,1280]{1,0:T(8,128)(4,1)S(1)} %copy-done.3, bf16[256,4,80]{0,2,1:T(8,128)(2,1)} %bitcast.39, bf16[1280,4,80]{0,2,1:T(8,128)(2,1)S(1)} %bitcast.32), kind=kOutput, calls=%fused_computation.22 | convolution fusion | flops 426068224 | bytes 2297856 | tf_op jit(solution)/shard_map/hqk,khd->qhd/dot_general | solution.py:77
  68.6 1.2 copy.33
  69.7 1.2 gather_fusion.1
  70.9 1.4 convolution_convert_fusion
  72.4 0.2 copy.32
  72.7 0.7 gather_fusion
  73.4 0.2 select_reduce_fusion
  73.6 34.7 %reduce-scatter.5.cloned.1.call-done = bf16[64,1280]{1,0:T(8,128)(2,1)} async-done(((bf16[256,1280]{1,0:T(8,128)(2,1)}), bf16[64,1280]{1,0:T(8,128)(2,1)}) %reduce-scatter.5.cloned.1.call-update) | async-done | bytes 163856 | tf_op jit(solution)/shard_map/reduce_scatter | solution.py:85
  108.3 1.1 fusion.18
  109.5 1.2 multiply_reduce_fusion
  110.7 1.4 convolution_convert_fusion.5
  112.1 0.8 copy.36
  112.9 0.1 fusion.25
  113.0 0.2 convert_element_type.93
  113.3 25.1 %reduce-scatter.7.cloned.1.call-done = bf16[160,64]{1,0:T(8,128)(2,1)} async-done(((bf16[640,64]{1,0:T(8,128)(2,1)}), bf16[160,64]{1,0:T(8,128)(2,1)}) %reduce-scatter.7.cloned.1.call-update) | async-done | bytes 20496
  138.4 1.0 convolution_convert_fusion.4
  139.3 0.1 copy.34
  139.5 0.3 fusion.19
  139.8 0.2 reshape.225
  140.0 28.9 %all_to_all.6 = bf16[128,2,240]{2,1,0:T(2,128)(2,1)S(1)} all-to-all(bf16[128,2,240]{2,1,0:T(2,128)(2,1)S(1)} %reshape.225), channel_id=1, replica_groups=mesh['seq'=128,'tp'=4] {'seq'}, dimensions={0} | all-to-all | bytes 245760 | tf_op jit(solution)/shard_map/all_to_all | solution.py:114
  168.8 0.2 reshape.226
  169.1 0.3 fusion.28
  169.4 0.1 reshape.197
  169.5 0.1 sub.55
  169.7 0.8 convolution_convert_fusion.6
  (59 shorter events, 0.7 us)
Async XLA Ops:
  6.5 104.2 %copy-start = (bf16[1280,640]{1,0:T(8,128)(2,1)S(1)}, bf16[1280,640]{1,0:T(8,128)(2,1)}, u32[]{:S(2)}) copy-start(bf16[1280,640]{1,0:T(8,128)(2,1)} %param.23) | copy-start | bytes 4915204
  6.5 12.1 %copy-start.10 = (f32[1280]{0:T(1024)S(1)}, f32[1280]{0:T(1024)}, u32[]{:S(2)}) copy-start(f32[1280]{0:T(1024)} %param.15) | copy-start | bytes 15364
  6.5 12.1 %copy-start.8 = (bf16[1280,320]{0,1:T(8,128)(2,1)S(1)}, bf16[1280,320]{0,1:T(8,128)(2,1)}, u32[]{:S(2)}) copy-start(bf16[1280,320]{0,1:T(8,128)(2,1)} %param.17) | copy-start | bytes 2457604
  6.5 101.8 %reduce-scatter.5.cloned.1.call-start = ((), (), s32[]{:S(2)}) async-start(), calls=%async_computation.3 | async-start | bytes 819200 | tf_op jit(solution)/shard_map/reduce_scatter | solution.py:85
  18.4 1.1 copy-start.9
  19.6 16.5 %copy-start.6 = (s32[256]{0:T(256)S(1)}, s32[256]{0:T(256)}, u32[]{:S(2)}) copy-start(s32[256]{0:T(256)} %param.20) | copy-start | bytes 3076
  19.6 16.5 %copy-start.7 = (s32[256]{0:T(256)S(1)}, s32[256]{0:T(256)}, u32[]{:S(2)}) copy-start(s32[256]{0:T(256)} %param.21) | copy-start | bytes 3076
  19.6 20.4 %copy-start.5 = (s32[64,4]{0,1:T(4,128)S(1)}, s32[64,4]{0,1:T(4,128)}, u32[]{:S(2)}) copy-start(s32[64,4]{0,1:T(4,128)} %param.24) | copy-start | bytes 3076
  20.9 38.4 %collective-permute-start = (bf16[256,640]{0,1:T(8,128)(2,1)}, bf16[256,640]{0,1:T(8,128)(2,1)}, u32[]{:S(2)}, u32[]{:S(2)}) collective-permute-start(bf16[256,640]{0,1:T(8,128)(2,1)} %get-tuple-element.23), channel_id=1, source_target_pairs={{0,4},{4,8},{8,12},{12,16},{16,20},{20,24},{24,28},{28,32},{32,36}... | collective-permute-start | bytes 983048 | tf_op jit(solution)/shard_map/ppermute | solution.py:14
  28.4 31.9 %collective-permute-start.1 = (bf16[256,640]{0,1:T(8,128)(2,1)}, bf16[256,640]{0,1:T(8,128)(2,1)S(1)}, u32[]{:S(2)}, u32[]{:S(2)}) collective-permute-start(bf16[256,640]{0,1:T(8,128)(2,1)} %get-tuple-element.23), channel_id=1, source_target_pairs={{0,8},{4,12},{8,16},{12,20},{16,24},{20,28},{24,32},{28,36},{32,40... | collective-permute-start | bytes 983048 | tf_op jit(solution)/shard_map/ppermute | solution.py:14
  32.4 28.0 %collective-permute-start.2 = (bf16[256,640]{0,1:T(8,128)(2,1)}, bf16[256,640]{0,1:T(8,128)(2,1)S(1)}, u32[]{:S(2)}, u32[]{:S(2)}) collective-permute-start(bf16[256,640]{0,1:T(8,128)(2,1)} %get-tuple-element.23), channel_id=1, source_target_pairs={{4,0},{8,4},{12,8},{16,12},{20,16},{24,20},{28,24},{32,28},{36,32}... | collective-permute-start | bytes 983048 | tf_op jit(solution)/shard_map/ppermute | solution.py:14
  34.7 25.7 %collective-permute-start.3 = (bf16[256,640]{0,1:T(8,128)(2,1)}, bf16[256,640]{0,1:T(8,128)(2,1)S(1)}, u32[]{:S(2)}, u32[]{:S(2)}) collective-permute-start(bf16[256,640]{0,1:T(8,128)(2,1)} %get-tuple-element.23), channel_id=1, source_target_pairs={{8,0},{12,4},{16,8},{20,12},{24,16},{28,20},{32,24},{36,28},{40,32... | collective-permute-start | bytes 983048 | tf_op jit(solution)/shard_map/ppermute | solution.py:14
  36.1 6.5 %collective-permute-start.4 = (s32[256]{0:T(256)S(1)}, s32[256]{0:T(256)S(1)}, u32[]{:S(2)}, u32[]{:S(2)}) collective-permute-start(s32[256]{0:T(256)S(1)} %get-tuple-element.20), channel_id=1, source_target_pairs={{0,4},{4,8},{8,12},{12,16},{16,20},{20,24},{24,28},{28,32},{32,36}... | collective-permute-start | bytes 3080 | tf_op jit(solution)/shard_map/ppermute | solution.py:14
  40.2 19.2 %copy-start.1 = (bf16[1280,640]{0,1:T(8,128)(2,1)S(1)}, bf16[1280,640]{0,1:T(8,128)(2,1)}, u32[]{:S(2)}) copy-start(bf16[1280,640]{0,1:T(8,128)(2,1)} %get-tuple-element.24) | copy-start | bytes 4915204
  42.6 4.7 %collective-permute-start.5 = (s32[256]{0:T(256)S(1)}, s32[256]{0:T(256)S(1)}, u32[]{:S(2)}, u32[]{:S(2)}) collective-permute-start(s32[256]{0:T(256)S(1)} %get-tuple-element.20), channel_id=1, source_target_pairs={{0,8},{4,12},{8,16},{12,20},{16,24},{20,28},{24,32},{28,36},{32,40... | collective-permute-start | bytes 3080 | tf_op jit(solution)/shard_map/ppermute | solution.py:14
  47.3 6.0 %collective-permute-start.6 = (s32[256]{0:T(256)S(1)}, s32[256]{0:T(256)S(1)}, u32[]{:S(2)}, u32[]{:S(2)}) collective-permute-start(s32[256]{0:T(256)S(1)} %get-tuple-element.20), channel_id=1, source_target_pairs={{4,0},{8,4},{12,8},{16,12},{20,16},{24,20},{28,24},{32,28},{36,32}... | collective-permute-start | bytes 3080 | tf_op jit(solution)/shard_map/ppermute | solution.py:14
  53.3 5.1 %collective-permute-start.7 = (s32[256]{0:T(256)S(1)}, s32[256]{0:T(256)S(1)}, u32[]{:S(2)}, u32[]{:S(2)}) collective-permute-start(s32[256]{0:T(256)S(1)} %get-tuple-element.20), channel_id=1, source_target_pairs={{8,0},{12,4},{16,8},{20,12},{24,16},{28,20},{32,24},{36,28},{40,32... | collective-permute-start | bytes 3080 | tf_op jit(solution)/shard_map/ppermute | solution.py:14
  60.5 1.0 copy-start.3
  68.6 2.3 %copy-start.2 = (bf16[320,1280]{1,0:T(8,128)(2,1)S(1)}, bf16[320,1280]{1,0:T(8,128)(2,1)}, u32[]{:S(2)}) copy-start(bf16[320,1280]{1,0:T(8,128)(2,1)} %param.19) | copy-start | bytes 2457604
  72.3 1.1 copy-start.11
  72.3 38.4 %copy-start.4 = (f32[1280]{0:T(1024)S(1)}, f32[1280]{0:T(1024)}, u32[]{:S(2)}) copy-start(f32[1280]{0:T(1024)} %param.22) | copy-start | bytes 15364
  72.3 66.1 %reduce-scatter.7.cloned.1.call-start = ((), (), s32[]{:S(2)}) async-start(), calls=%async_computation.4 | async-start | bytes 204800
Sparse Core Ops, SparseCore 0:
  72.4 35.8 reduce-scatter.4
  113.0 25.2 reduce-scatter.6
where the time goes:
time: 178 us; the launch traced here: 177 us
  waiting for transfers between devices  68.4 us (38%)
  blocking collectives  40.5 us (23%)
  starting transfers between devices  26.1 us (15%)
  matrix products  15.1 us (8%)
  between operations  13.8 us (8%)
  local copies, waits for them, and re-layouts  7.86 us (4%)
  other arithmetic  5.42 us (3%)
    reduce_scatter x1, waiting for transfers between devices, body(): lax.psum_scatter(partial_sum.astype(jnp.bfloat16), 'tp', scatter_dimensio...  34.7 us
    all_to_all x1, blocking collectives, body(): lax.all_to_all(send_buf, 'seq', 0, 0, tiled=True)  28.9 us
    ppermute x8, starting transfers between devices, from_behind(): return lax.ppermute(shard, axis, pairs)  26.1 us
    unnamed x3, waiting for transfers between devices  25.1 us
    all_gather x1, blocking collectives, body(): gathered = lax.all_gather(tokens, 'tp', axis=1, tiled=True)  11.7 us
    ppermute x8, waiting for transfers between devices, from_behind(): return lax.ppermute(shard, axis, pairs)  8.52 us
    dot_general x1, matrix products, body(): jnp.einsum('hqk,khd->qhd', weights, value_heads, preferred_element_type=j...  4.14 us
  transfers between devices with their start and end apart: 10, of which 5 were waited for; matrix products, arithmetic and copies ran while one was open for 4% of the time, Pallas kernels for 0%

commit v1 on v0

--- a/solution.py
+++ b/solution.py
@@ -41,7 +41,22 @@
     heads_here = local_width // HD
     tp_size = lax.axis_size("tp")
     seq_size = lax.axis_size("seq")
-    gathered = lax.all_gather(tokens, "tp", axis=1, tiled=True)
+    ways, here, step = (lax.axis_size("tp"), lax.axis_index("tp"), tokens.shape[1])
+    dims = [n * ways if d == 1 else n for d, n in enumerate(tokens.shape)]
+    gathered = lax.dynamic_update_slice_in_dim(
+        jnp.zeros(dims, tokens.dtype), tokens, here * step, axis=1
+    )
+    going_up = going_down = tokens
+    for far in range(1, ways // 2 + 1):
+        going_up = lax.ppermute(going_up, "tp", [(d, (d + 1) % ways) for d in range(ways)])
+        gathered = lax.dynamic_update_slice_in_dim(
+            gathered, going_up, (here - far) % ways * step, axis=1
+        )
+        if 2 * far < ways:
+            going_down = lax.ppermute(going_down, "tp", [(d, (d - 1) % ways) for d in range(ways)])
+            gathered = lax.dynamic_update_slice_in_dim(
+                gathered, going_down, (here + far) % ways * step, axis=1
+            )
     normed = layer_norm(gathered, first_gain).astype(jnp.bfloat16)
     queries = jnp.dot(normed, w_query, preferred_element_type=jnp.float32).astype(jnp.bfloat16)
     key_rows = jnp.dot(normed, w_key, preferred_element_type=jnp.float32).astype(jnp.bfloat16)

time: 178 us -> 181 us (1.017)
  blocking collectives: 40.5 us -> 28.9 us
  local copies, waits for them, and re-layouts: 7.86 us -> 17.9 us
  starting transfers between devices: 26.1 us -> 35 us
  waiting for transfers between devices: 68.4 us -> 63.9 us
    all_gather x1 -> x0, blocking collectives: 11.7 us -> none  [body(): gathered = lax.all_gather(tokens, 'tp', axis=1, tiled=True)]
    dynamic_update_slice x0 -> x4, local copies, waits for them, and re-layouts: none -> 10.4 us  [the longest x2 4.64 us: body(): lax.dynamic_update_slice_in_dim(gathered, going_up, (here - far) % ways *...]
    ppermute x0 -> x3, starting transfers between devices: none -> 9.66 us  [the longest x2 6.48 us: body(): lax.ppermute(going_up, 'tp', [(d, (d + 1) % ways) for d in range(ways)])]
    reduce_scatter x1, waiting for transfers between devices: 34.7 us -> 26.7 us  [body(): lax.psum_scatter(partial_sum.astype(jnp.bfloat16), 'tp', scatter_dimensio...]
    ppermute x8, waiting for transfers between devices: 8.52 us -> 11.8 us  [from_behind(): return lax.ppermute(shard, axis, pairs)]
  transfers between devices with their start and end apart: 10 -> 13, of which waited for: 5 -> 7; matrix products, arithmetic and copies ran while one was open for 4% -> 7% of each run, Pallas kernels for 0% -> 0%
where the time goes in v1:
time: 181 us; the launch traced here: 180 us
  waiting for transfers between devices  63.9 us (35%)
  starting transfers between devices  35 us (19%)
  blocking collectives  28.9 us (16%)
  local copies, waits for them, and re-layouts  17.9 us (10%)
  matrix products  15.1 us (8%)
  between operations  14 us (8%)
  other arithmetic  5.27 us (3%)
    all_to_all x1, blocking collectives, body(): lax.all_to_all(send_buf, 'seq', 0, 0, tiled=True)  28.9 us
    reduce_scatter x1, waiting for transfers between devices, body(): lax.psum_scatter(partial_sum.astype(jnp.bfloat16), 'tp', scatter_dimensio...  26.7 us
    ppermute x8, starting transfers between devices, from_behind(): return lax.ppermute(shard, axis, pairs)  25.1 us
    unnamed x3, waiting for transfers between devices  25.1 us
    ppermute x8, waiting for transfers between devices, from_behind(): return lax.ppermute(shard, axis, pairs)  11.8 us
    ppermute x2, starting transfers between devices, body(): lax.ppermute(going_up, 'tp', [(d, (d + 1) % ways) for d in range(ways)])  6.48 us
    dynamic_update_slice x2, local copies, waits for them, and re-layouts, body(): lax.dynamic_update_slice_in_dim(gathered, going_up, (here - far) % ways *...  4.64 us
    dot_general x1, matrix products, body(): jnp.einsum('hqk,khd->qhd', weights, value_heads, preferred_element_type=j...  4.14 us
  transfers between devices with their start and end apart: 13, of which 7 were waited for; matrix products, arithmetic and copies ran while one was open for 7% of the time, Pallas kernels for 0%

profile of v1, /device:TPU:1, one launch (start us, length us, event | category | flops | bytes accessed | tf_op | source)
XLA Modules:
  0.0 180.0 jit_solution(8354308909580425365)
XLA Ops:
  6.5 1.2 copy.40
  7.7 3.9 %collective-permute-start = (bf16[256,320]{1,0:T(8,128)(2,1)S(1)}, bf16[256,320]{1,0:T(8,128)(2,1)S(1)}, u32[]{:S(2)}, u32[]{:S(2)}) collective-permute-start(bf16[256,320]{1,0:T(8,128)(2,1)S(1)} %copy.40), channel_id=1, source_target_pairs={{0,1},{1,2},{2,3},{3,0},{4,5},{5,6},{6,7},{7,4},{8,9},{9,10},{10,1... | collective-permute-start | bytes 491528 | tf_op jit(solution)/shard_map/ppermute | solution.py:51
  11.7 3.2 %collective-permute-start.1 = (bf16[256,320]{1,0:T(8,128)(2,1)S(1)}, bf16[256,320]{1,0:T(8,128)(2,1)S(1)}, u32[]{:S(2)}, u32[]{:S(2)}) collective-permute-start(bf16[256,320]{1,0:T(8,128)(2,1)S(1)} %copy.40), channel_id=1, source_target_pairs={{0,3},{1,0},{2,1},{3,2},{4,7},{5,4},{6,5},{7,6},{8,11},{9,8},{10,9... | collective-permute-start | bytes 491528 | tf_op jit(solution)/shard_map/ppermute | solution.py:56
  14.9 0.7 constant_dynamic-update-slice_fusion.5
  15.6 5.3 %collective-permute-start.7 = (s32[256]{0:T(256)S(1)}, s32[256]{0:T(256)S(1)}, u32[]{:S(2)}, u32[]{:S(2)}) collective-permute-start(s32[256]{0:T(256)S(1)} %get-tuple-element.20), channel_id=1, source_target_pairs={{0,4},{4,8},{8,12},{12,16},{16,20},{20,24},{24,28},{28,32},{32,36}... | collective-permute-start | bytes 3080 | tf_op jit(solution)/shard_map/ppermute | solution.py:14
  20.9 4.0 %collective-permute-start.8 = (s32[256]{0:T(256)S(1)}, s32[256]{0:T(256)S(1)}, u32[]{:S(2)}, u32[]{:S(2)}) collective-permute-start(s32[256]{0:T(256)S(1)} %get-tuple-element.20), channel_id=1, source_target_pairs={{0,8},{4,12},{8,16},{12,20},{16,24},{20,28},{24,32},{28,36},{32,40... | collective-permute-start | bytes 3080 | tf_op jit(solution)/shard_map/ppermute | solution.py:14
  24.9 2.0 %collective-permute-start.9 = (s32[256]{0:T(256)S(1)}, s32[256]{0:T(256)S(1)}, u32[]{:S(2)}, u32[]{:S(2)}) collective-permute-start(s32[256]{0:T(256)S(1)} %get-tuple-element.20), channel_id=1, source_target_pairs={{4,0},{8,4},{12,8},{16,12},{20,16},{24,20},{28,24},{32,28},{36,32}... | collective-permute-start | bytes 3080 | tf_op jit(solution)/shard_map/ppermute | solution.py:14
  26.9 0.7 fusion.66
  27.9 2.6 %dynamic_update_slice.12 = bf16[256,1280]{1,0:T(8,128)(2,1)S(1)} dynamic-update-slice(bf16[256,1280]{1,0:T(8,128)(2,1)S(1)} %broadcast_in_dim.47, bf16[256,320]{1,0:T(8,128)(2,1)S(1)} %copy.40, s32[]{:T(128)} %constant.116.clone.1, s32[]{:T(128)S(6)} %select_n.81) | dynamic-update-slice | bytes 327684 | tf_op jit(solution)/shard_map/dynamic_update_slice | solution.py:46
  30.5 1.3 collective-permute-start.10
  31.8 2.5 %collective-permute-start.2 = (bf16[256,320]{1,0:T(8,128)(2,1)S(1)}, bf16[256,320]{1,0:T(8,128)(2,1)S(1)}, u32[]{:S(2)}, u32[]{:S(2)}) collective-permute-start(bf16[256,320]{1,0:T(8,128)(2,1)S(1)} %collective-permute-done), channel_id=1, source_target_pairs={{0,1},{1,2},{2,3},{3,0},{4,5},{5,6},{6,7},{7,4},{8,9},{9,10},{10,1... | collective-permute-start | bytes 491528 | tf_op jit(solution)/shard_map/ppermute | solution.py:51
  34.4 1.2 collective-permute-done.10
  35.6 2.4 %dynamic_update_slice.13 = bf16[256,1280]{1,0:T(8,128)(2,1)S(1)} dynamic-update-slice(bf16[256,1280]{1,0:T(8,128)(2,1)S(1)} %dynamic_update_slice.12, bf16[256,320]{1,0:T(8,128)(2,1)S(1)} %collective-permute-done, s32[]{:T(128)} %constant.116.clone.1, s32[]{:T(128)S(6)} %select_n.83) | dynamic-update-slice | bytes 327684 | tf_op jit(solution)/shard_map/dynamic_update_slice | solution.py:52
  38.0 3.2 %dynamic_update_slice.14 = bf16[256,1280]{1,0:T(8,128)(2,1)S(1)} dynamic-update-slice(bf16[256,1280]{1,0:T(8,128)(2,1)S(1)} %dynamic_update_slice.13, bf16[256,320]{1,0:T(8,128)(2,1)S(1)} %collective-permute-done.1, s32[]{:T(128)} %constant.116.clone.1, s32[]{:T(128)S(6)} %select_n.85) | dynamic-update-slice | bytes 327684 | tf_op jit(solution)/shard_map/dynamic_update_slice | solution.py:57
  41.3 0.3 collective-permute-done.2
  41.5 2.2 %dynamic_update_slice.15 = bf16[256,1280]{1,0:T(8,128)(2,1)S(1)} dynamic-update-slice(bf16[256,1280]{1,0:T(8,128)(2,1)S(1)} %dynamic_update_slice.14, bf16[256,320]{1,0:T(8,128)(2,1)S(1)} %collective-permute-done.2, s32[]{:T(128)} %constant.116.clone.1, s32[]{:T(128)S(6)} %select_n.87) | dynamic-update-slice | bytes 327684 | tf_op jit(solution)/shard_map/dynamic_update_slice | solution.py:52
  44.0 0.3 fusion.9
  44.3 1.7 convolution_convert_fusion.3
  46.0 0.5 convolution_convert_fusion.2
  46.6 5.2 %collective-permute-start.3 = (bf16[256,640]{0,1:T(8,128)(2,1)S(1)}, bf16[256,640]{0,1:T(8,128)(2,1)S(1)}, u32[]{:S(2)}, u32[]{:S(2)}) collective-permute-start(bf16[256,640]{0,1:T(8,128)(2,1)S(1)} %get-tuple-element.23), channel_id=1, source_target_pairs={{0,4},{4,8},{8,12},{12,16},{16,20},{20,24},{24,28},{28,32},{32,36}... | collective-permute-start | bytes 983048 | tf_op jit(solution)/shard_map/ppermute | solution.py:14
  51.8 0.2 fusion.12
  52.0 4.1 %collective-permute-start.4 = (bf16[256,640]{0,1:T(8,128)(2,1)S(1)}, bf16[256,640]{0,1:T(8,128)(2,1)S(1)}, u32[]{:S(2)}, u32[]{:S(2)}) collective-permute-start(bf16[256,640]{0,1:T(8,128)(2,1)S(1)} %get-tuple-element.23), channel_id=1, source_target_pairs={{0,8},{4,12},{8,16},{12,20},{16,24},{20,28},{24,32},{28,36},{32,40... | collective-permute-start | bytes 983048 | tf_op jit(solution)/shard_map/ppermute | solution.py:14
  56.2 1.9 %collective-permute-start.5 = (bf16[256,640]{0,1:T(8,128)(2,1)S(1)}, bf16[256,640]{0,1:T(8,128)(2,1)S(1)}, u32[]{:S(2)}, u32[]{:S(2)}) collective-permute-start(bf16[256,640]{0,1:T(8,128)(2,1)S(1)} %get-tuple-element.23), channel_id=1, source_target_pairs={{4,0},{8,4},{12,8},{16,12},{20,16},{24,20},{28,24},{32,28},{36,32}... | collective-permute-start | bytes 983048 | tf_op jit(solution)/shard_map/ppermute | solution.py:14
  58.1 1.3 collective-permute-start.6
  59.4 1.2 convolution_convert_fusion.1
  60.6 2.2 %collective-permute-done.4 = bf16[256,640]{0,1:T(8,128)(2,1)S(1)} collective-permute-done((bf16[256,640]{0,1:T(8,128)(2,1)S(1)}, bf16[256,640]{0,1:T(8,128)(2,1)S(1)}, u32[]{:S(2)}, u32[]{:S(2)}) %collective-permute-start.4) | collective-permute-done | bytes 327712 | tf_op jit(solution)/shard_map/ppermute | solution.py:14
  62.8 2.4 %collective-permute-done.5 = bf16[256,640]{0,1:T(8,128)(2,1)S(1)} collective-permute-done((bf16[256,640]{0,1:T(8,128)(2,1)S(1)}, bf16[256,640]{0,1:T(8,128)(2,1)S(1)}, u32[]{:S(2)}, u32[]{:S(2)}) %collective-permute-start.5) | collective-permute-done | bytes 327712 | tf_op jit(solution)/shard_map/ppermute | solution.py:14
  65.3 6.0 %collective-permute-done.6 = bf16[256,640]{0,1:T(8,128)(2,1)S(1)} collective-permute-done((bf16[256,640]{0,1:T(8,128)(2,1)S(1)}, bf16[256,640]{0,1:T(8,128)(2,1)S(1)}, u32[]{:S(2)}, u32[]{:S(2)}) %collective-permute-start.6) | collective-permute-done | bytes 327712 | tf_op jit(solution)/shard_map/ppermute | solution.py:14
  71.2 1.0 fusion.54
  72.2 2.9 %exponential_reduce_fusion = f32[4,256]{1,0:T(4,128)S(1)} fusion(pred[256,1280]{1,0:T(8,128)(4,1)S(1)} %fusion.12, bf16[256,4,80]{0,2,1:T(8,128)(2,1)} %bitcast.38, bf16[1280,4,80]{0,2,1:T(8,128)(2,1)S(1)} %bitcast.31), kind=kOutput, calls=%fused_computation.6 | convolution fusion | flops 214959360 | bytes 1314816 | tf_op jit(solution)/shard_map/sub | solution.py:89
  75.2 4.1 %fusion.13 = bf16[4,80,256]{2,1,0:T(8,128)(2,1)} fusion(bf16[1280,4,80]{0,2,1:T(8,128)(2,1)} %bitcast.33, f32[4,256]{1,0:T(4,128)S(1)} %exponential_reduce_fusion, pred[256,1280]{1,0:T(8,128)(4,1)S(1)} %fusion.12, bf16[256,4,80]{0,2,1:T(8,128)(2,1)} %bitcast.39, bf16[1280,4,80]{0,2,1:T(8,128)(2,1)S(1)} %bitcast.32), kind=kOutput, calls=%fused_computation.22 | convolution fusion | flops 426068224 | bytes 2297856 | tf_op jit(solution)/shard_map/hqk,khd->qhd/dot_general | solution.py:92
  79.3 1.2 copy.43
  80.5 1.2 gather_fusion.1
  81.7 1.4 convolution_convert_fusion
  83.1 0.2 reduce-scatter.7.cloned.1.call-start
  83.6 0.7 gather_fusion
  84.3 26.7 %reduce-scatter.5.cloned.1.call-done = bf16[64,1280]{1,0:T(8,128)(2,1)} async-done(((bf16[256,1280]{1,0:T(8,128)(2,1)}), bf16[64,1280]{1,0:T(8,128)(2,1)}) %reduce-scatter.5.cloned.1.call-update) | async-done | bytes 163856 | tf_op jit(solution)/shard_map/reduce_scatter | solution.py:100
  111.1 1.1 fusion.18
  112.2 1.2 multiply_reduce_fusion
  113.4 1.4 convolution_convert_fusion.5
  114.8 0.8 copy.46
  115.8 0.2 convert_element_type.93
  116.0 25.1 %reduce-scatter.7.cloned.1.call-done = bf16[160,64]{1,0:T(8,128)(2,1)} async-done(((bf16[640,64]{1,0:T(8,128)(2,1)}), bf16[160,64]{1,0:T(8,128)(2,1)}) %reduce-scatter.7.cloned.1.call-update) | async-done | bytes 20496
  141.1 1.0 convolution_convert_fusion.4
  142.2 0.3 fusion.19
  142.7 28.9 %all_to_all.6 = bf16[128,2,240]{2,1,0:T(2,128)(2,1)S(1)} all-to-all(bf16[128,2,240]{2,1,0:T(2,128)(2,1)S(1)} %reshape.225), channel_id=1, replica_groups=mesh['seq'=128,'tp'=4] {'seq'}, dimensions={0} | all-to-all | bytes 245760 | tf_op jit(solution)/shard_map/all_to_all | solution.py:129
  171.8 0.3 fusion.28
  172.4 0.8 convolution_convert_fusion.6
  (61 shorter events, 1.9 us)
Async XLA Ops:
  6.5 106.9 %copy-start = (bf16[1280,640]{1,0:T(8,128)(2,1)S(1)}, bf16[1280,640]{1,0:T(8,128)(2,1)}, u32[]{:S(2)}) copy-start(bf16[1280,640]{1,0:T(8,128)(2,1)} %param.23) | copy-start | bytes 4915204
  6.5 104.5 %reduce-scatter.5.cloned.1.call-start = ((), (), s32[]{:S(2)}) async-start(), calls=%async_computation.3 | async-start | bytes 819200 | tf_op jit(solution)/shard_map/reduce_scatter | solution.py:100
  7.7 24.1 %collective-permute-start = (bf16[256,320]{1,0:T(8,128)(2,1)S(1)}, bf16[256,320]{1,0:T(8,128)(2,1)S(1)}, u32[]{:S(2)}, u32[]{:S(2)}) collective-permute-start(bf16[256,320]{1,0:T(8,128)(2,1)S(1)} %copy.40), channel_id=1, source_target_pairs={{0,1},{1,2},{2,3},{3,0},{4,5},{5,6},{6,7},{7,4},{8,9},{9,10},{10,1... | collective-permute-start | bytes 491528 | tf_op jit(solution)/shard_map/ppermute | solution.py:51
  11.7 26.3 %collective-permute-start.1 = (bf16[256,320]{1,0:T(8,128)(2,1)S(1)}, bf16[256,320]{1,0:T(8,128)(2,1)S(1)}, u32[]{:S(2)}, u32[]{:S(2)}) collective-permute-start(bf16[256,320]{1,0:T(8,128)(2,1)S(1)} %copy.40), channel_id=1, source_target_pairs={{0,3},{1,0},{2,1},{3,2},{4,7},{5,4},{6,5},{7,6},{8,11},{9,8},{10,9... | collective-permute-start | bytes 491528 | tf_op jit(solution)/shard_map/ppermute | solution.py:56
  15.6 14.9 %collective-permute-start.7 = (s32[256]{0:T(256)S(1)}, s32[256]{0:T(256)S(1)}, u32[]{:S(2)}, u32[]{:S(2)}) collective-permute-start(s32[256]{0:T(256)S(1)} %get-tuple-element.20), channel_id=1, source_target_pairs={{0,4},{4,8},{8,12},{12,16},{16,20},{20,24},{24,28},{28,32},{32,36}... | collective-permute-start | bytes 3080 | tf_op jit(solution)/shard_map/ppermute | solution.py:14
  20.9 10.9 %collective-permute-start.8 = (s32[256]{0:T(256)S(1)}, s32[256]{0:T(256)S(1)}, u32[]{:S(2)}, u32[]{:S(2)}) collective-permute-start(s32[256]{0:T(256)S(1)} %get-tuple-element.20), channel_id=1, source_target_pairs={{0,8},{4,12},{8,16},{12,20},{16,24},{20,28},{24,32},{28,36},{32,40... | collective-permute-start | bytes 3080 | tf_op jit(solution)/shard_map/ppermute | solution.py:14
  24.9 9.5 %collective-permute-start.9 = (s32[256]{0:T(256)S(1)}, s32[256]{0:T(256)S(1)}, u32[]{:S(2)}, u32[]{:S(2)}) collective-permute-start(s32[256]{0:T(256)S(1)} %get-tuple-element.20), channel_id=1, source_target_pairs={{4,0},{8,4},{12,8},{16,12},{20,16},{24,20},{28,24},{32,28},{36,32}... | collective-permute-start | bytes 3080 | tf_op jit(solution)/shard_map/ppermute | solution.py:14
  27.8 16.5 %copy-start.6 = (f32[1280]{0:T(1024)S(1)}, f32[1280]{0:T(1024)}, u32[]{:S(2)}) copy-start(f32[1280]{0:T(1024)} %param.15) | copy-start | bytes 15364
  30.5 5.2 %collective-permute-start.10 = (s32[256]{0:T(256)S(1)}, s32[256]{0:T(256)S(1)}, u32[]{:S(2)}, u32[]{:S(2)}) collective-permute-start(s32[256]{0:T(256)S(1)} %get-tuple-element.20), channel_id=1, source_target_pairs={{8,0},{12,4},{16,8},{20,12},{24,16},{28,20},{32,24},{36,28},{40,32... | collective-permute-start | bytes 3080 | tf_op jit(solution)/shard_map/ppermute | solution.py:14
  31.8 9.7 %collective-permute-start.2 = (bf16[256,320]{1,0:T(8,128)(2,1)S(1)}, bf16[256,320]{1,0:T(8,128)(2,1)S(1)}, u32[]{:S(2)}, u32[]{:S(2)}) collective-permute-start(bf16[256,320]{1,0:T(8,128)(2,1)S(1)} %collective-permute-done), channel_id=1, source_target_pairs={{0,1},{1,2},{2,3},{3,0},{4,5},{5,6},{6,7},{7,4},{8,9},{9,10},{10,1... | collective-permute-start | bytes 491528 | tf_op jit(solution)/shard_map/ppermute | solution.py:51
  43.9 2.0 %copy-start.4 = (bf16[1280,320]{0,1:T(8,128)(2,1)S(1)}, bf16[1280,320]{0,1:T(8,128)(2,1)}, u32[]{:S(2)}) copy-start(bf16[1280,320]{0,1:T(8,128)(2,1)} %param.18) | copy-start | bytes 2457604
  46.0 13.4 %copy-start.5 = (bf16[1280,320]{0,1:T(8,128)(2,1)S(1)}, bf16[1280,320]{0,1:T(8,128)(2,1)}, u32[]{:S(2)}) copy-start(bf16[1280,320]{0,1:T(8,128)(2,1)} %param.16) | copy-start | bytes 2457604
  46.6 14.0 %collective-permute-start.3 = (bf16[256,640]{0,1:T(8,128)(2,1)S(1)}, bf16[256,640]{0,1:T(8,128)(2,1)S(1)}, u32[]{:S(2)}, u32[]{:S(2)}) collective-permute-start(bf16[256,640]{0,1:T(8,128)(2,1)S(1)} %get-tuple-element.23), channel_id=1, source_target_pairs={{0,4},{4,8},{8,12},{12,16},{16,20},{20,24},{24,28},{28,32},{32,36}... | collective-permute-start | bytes 983048 | tf_op jit(solution)/shard_map/ppermute | solution.py:14
  52.0 10.8 %collective-permute-start.4 = (bf16[256,640]{0,1:T(8,128)(2,1)S(1)}, bf16[256,640]{0,1:T(8,128)(2,1)S(1)}, u32[]{:S(2)}, u32[]{:S(2)}) collective-permute-start(bf16[256,640]{0,1:T(8,128)(2,1)S(1)} %get-tuple-element.23), channel_id=1, source_target_pairs={{0,8},{4,12},{8,16},{12,20},{16,24},{20,28},{24,32},{28,36},{32,40... | collective-permute-start | bytes 983048 | tf_op jit(solution)/shard_map/ppermute | solution.py:14
  56.2 9.1 %collective-permute-start.5 = (bf16[256,640]{0,1:T(8,128)(2,1)S(1)}, bf16[256,640]{0,1:T(8,128)(2,1)S(1)}, u32[]{:S(2)}, u32[]{:S(2)}) collective-permute-start(bf16[256,640]{0,1:T(8,128)(2,1)S(1)} %get-tuple-element.23), channel_id=1, source_target_pairs={{4,0},{8,4},{12,8},{16,12},{20,16},{24,20},{28,24},{32,28},{36,32}... | collective-permute-start | bytes 983048 | tf_op jit(solution)/shard_map/ppermute | solution.py:14
  58.1 13.1 %collective-permute-start.6 = (bf16[256,640]{0,1:T(8,128)(2,1)S(1)}, bf16[256,640]{0,1:T(8,128)(2,1)S(1)}, u32[]{:S(2)}, u32[]{:S(2)}) collective-permute-start(bf16[256,640]{0,1:T(8,128)(2,1)S(1)} %get-tuple-element.23), channel_id=1, source_target_pairs={{8,0},{12,4},{16,8},{20,12},{24,16},{28,20},{32,24},{36,28},{40,32... | collective-permute-start | bytes 983048 | tf_op jit(solution)/shard_map/ppermute | solution.py:14
  79.3 2.4 %copy-start.1 = (bf16[320,1280]{1,0:T(8,128)(2,1)S(1)}, bf16[320,1280]{1,0:T(8,128)(2,1)}, u32[]{:S(2)}) copy-start(bf16[320,1280]{1,0:T(8,128)(2,1)} %param.19) | copy-start | bytes 2457604
  80.5 2.8 %copy-start.3 = (s32[64,4]{0,1:T(4,128)S(1)}, s32[64,4]{0,1:T(4,128)}, u32[]{:S(2)}) copy-start(s32[64,4]{0,1:T(4,128)} %param.24) | copy-start | bytes 3076
  80.5 2.9 %copy-start.7 = (s32[64]{0:T(128)S(1)}, s32[64]{0:T(128)}, u32[]{:S(2)}) copy-start(s32[64]{0:T(128)} %param.25) | copy-start | bytes 772
  83.1 30.4 %copy-start.2 = (f32[1280]{0:T(1024)S(1)}, f32[1280]{0:T(1024)}, u32[]{:S(2)}) copy-start(f32[1280]{0:T(1024)} %param.22) | copy-start | bytes 15364
  83.1 58.0 %reduce-scatter.7.cloned.1.call-start = ((), (), s32[]{:S(2)}) async-start(), calls=%async_computation.4 | async-start | bytes 204800
Sparse Core Ops, SparseCore 0:
  83.2 27.8 reduce-scatter.4
  115.8 25.2 reduce-scatter.6
